TPU v7x, 32 devices: a whole 2x2x4 slice. The times are simulated.
32 devices in a mesh: test: 4 (over z), cell: 8 (over y, x, core).
Axes of the slice: x: 2, y: 2, z: 4, core: 2. Of those that a mesh axis runs over, the one named last changes fastest.
Arguments:
- log_perm: float32 [128, 16, 256], P('cell'), may hold values from -1 to 1
- panel: float32 [8, 128, 16, 256], P('test', 'cell'), may hold values from -4 to 4
- wells: int32 [4, 8], P('test'), may hold values from 0 to 524287
- rates: float32 [4, 8], P('test'), may hold values from 1 to 10
- recharge: float32 [4, 128, 16, 256], P('test', 'cell'), may hold values from 0.25 to 4
- gauge: float32 [128, 16, 256], P('cell'), may hold values from 0.25 to 4
Outputs:
- hessian_panel: float32 [8, 128, 16, 256], P('test', 'cell')
Inputs may be any that keep to these rules, and one draw needn't show every extreme that they name: `wells`: each entry names a cell of the whole grid, numbered x * 16 * 256 + y * 256 + z; a test may name a cell more than once.
All inputs are finite; a program needn't handle non-finite values.
Results may differ from a plain program's by a relative error of at most 0.0001.
Values sent between devices are 32-bit elements; how exact they have to be, the bound alone decides.
No kernel may reach another device: no remote copies, remote signals or barrier semaphores. Data moves between devices by JAX's collectives and lax.ppermute only.
A program may use at most 64 MiB of HBM per device.

v0:
```python
import math

import jax
import jax.numpy as jnp
import numpy as np
from jax import lax
from jax.sharding import PartitionSpec as P

CHEB = 4


storage = 0.02


def with_halo(cells, sides, width):
    for axis, dim in sides:
        count = lax.axis_size(axis)
        ends = count - 1
        head = lax.slice_in_dim(cells, 0, width, axis=dim)
        tail = lax.slice_in_dim(cells, cells.shape[dim] - width, cells.shape[dim], axis=dim)
        cells = jnp.concatenate(
            [
                lax.ppermute(tail, axis, [(i, (i + 1) % count) for i in range(ends)]),
                cells,
                lax.ppermute(head, axis, [((i + 1) % count, i) for i in range(ends)]),
            ],
            axis=dim,
        )
    return cells


def cheb_table(count):
    highest = storage + 12.0 * math.e
    theta = 0.5 * (highest + storage)
    spread = 0.5 * (highest - storage)
    sigma = theta / spread
    rho = 1.0 / sigma
    keeps = []
    pushes = []
    for turn in range(count):
        after = 1.0 / (2.0 * sigma - rho)
        keeps.append(after * rho)
        pushes.append(2.0 * after / spread)
        rho = after
    return (1.0 / theta, keeps, pushes)


def neighbours(field, back):
    axis = field.ndim - back
    widths = [(0, 0)] * field.ndim
    widths[axis] = (1, 1)
    padded = jnp.pad(field, widths)
    length = field.shape[axis]
    return (
        lax.slice_in_dim(padded, 2, length + 2, axis=axis),
        lax.slice_in_dim(padded, 0, length, axis=axis),
    )


def diffuse(weight_ext, field_ext):
    weight = weight_ext[..., 1:-1, :, :]
    field = field_ext[..., 1:-1, :, :]
    total = 0.5 * (weight + weight_ext[..., 2:, :, :]) * (field - field_ext[..., 2:, :, :])
    total = total + 0.5 * (weight + weight_ext[..., :-2, :, :]) * (
        field - field_ext[..., :-2, :, :]
    )
    for back in (2, 1):
        weight_up, weight_down = neighbours(weight, back)
        field_up, field_down = neighbours(field, back)
        total = (
            total
            + 0.5 * (weight + weight_up) * (field - field_up)
            + 0.5 * (weight + weight_down) * (field - field_down)
        )
    return total


def pairs(left_ext, right_ext):
    left = left_ext[..., 1:-1, :, :]
    right = right_ext[..., 1:-1, :, :]
    total = (left - left_ext[..., 2:, :, :]) * (right - right_ext[..., 2:, :, :])
    total = total + (left - left_ext[..., :-2, :, :]) * (right - right_ext[..., :-2, :, :])
    for back in (2, 1):
        left_up, left_down = neighbours(left, back)
        right_up, right_down = neighbours(right, back)
        total = (
            total
            + (left - left_up) * (right - right_up)
            + (left - left_down) * (right - right_down)
        )
    return total


def rims(field):
    return with_halo(field, (("cell", 1),), 1)


def shards(log_perm, panel, wells, rates, recharge, gauge):
    place = lax.axis_index("cell")
    slab, rows_y, depth_z = log_perm.shape
    tests_here, well_count = wells.shape
    first, keeps, pushes = cheb_table(CHEB)
    keep_table = jnp.asarray(np.array(keeps, np.float32))
    push_table = jnp.asarray(np.array(pushes, np.float32))
    columns = lax.all_gather(panel, "test", axis=0, tiled=True)
    columns_all = columns.shape[0]
    perm = jnp.exp(log_perm)
    stacked = jnp.concatenate([perm[None], perm[None] * columns], axis=0)
    coeff_ext = with_halo(stacked, (("cell", 1),), 2)
    perm_ext = coeff_ext[0]
    scaled_ext = coeff_ext[1:, 1:-1]
    cells = slab * rows_y * depth_z
    flat = place * cells + jnp.arange(cells, dtype=jnp.int32)
    hits = wells[:, :, None] == flat[None, None, :]
    points = jnp.sum(jnp.where(hits, rates[:, :, None], 0.0), axis=1).reshape(
        tests_here, slab, rows_y, depth_z
    )
    counts = jnp.sum(hits.astype(jnp.float32), axis=1).reshape(tests_here, slab, rows_y, depth_z)
    source = recharge + points
    observe = gauge[None] + counts

    def solve(right_side):
        solution = jnp.zeros_like(right_side)
        residual = right_side
        direction = right_side * first

        def sweep(turn, carry):
            solution, residual, direction = carry
            extended = with_halo(direction, (("cell", 1),), 1)
            image = storage * direction + diffuse(perm_ext[1:-1], extended)
            solution = solution + direction
            residual = residual - image
            direction = keep_table[turn] * direction + push_table[turn] * residual
            return (solution, residual, direction)

        solution, residual, direction = lax.fori_loop(
            0, CHEB, sweep, (solution, residual, direction)
        )
        return solution + direction

    state = solve(source)
    state_ext = rims(state)
    forcing = -diffuse(scaled_ext, state_ext[:, None])
    forcing = forcing.reshape(tests_here * columns_all, slab, rows_y, depth_z)
    change = solve(forcing)
    weighted = (
        change.reshape(tests_here, columns_all, slab, rows_y, depth_z) * observe[:, None]
    ).reshape(tests_here * columns_all, slab, rows_y, depth_z)
    adjoint = solve(weighted)
    adjoint_ext = rims(adjoint).reshape(tests_here, columns_all, slab + 2, rows_y, depth_z)
    contrib = jnp.sum(pairs(state_ext[:, None], adjoint_ext), axis=0)
    partial_value = -0.5 * perm[None] * contrib
    total = lax.psum(partial_value, "test")
    share = panel.shape[0]
    owned = lax.dynamic_slice_in_dim(total, lax.axis_index("test") * share, share, 0)
    return owned


def solution(mesh):
    return jax.shard_map(
        shards,
        mesh=mesh,
        in_specs=(
            P("cell", None, None),
            P("test", "cell", None, None),
            P("test", None),
            P("test", None),
            P("test", "cell", None, None),
            P("cell", None, None),
        ),
        out_specs=P("test", "cell", None, None),
        check_vma=False,
    )
```

profile of v0, /device:TPU:11, one launch (start us, length us, event | category | flops | bytes accessed | tf_op | source)
XLA Modules:
  0.0 405.3 jit_solution(683576134354521020)
XLA Ops:
  9.1 44.8 %all-gather.2.cloned.1.call-done = f32[8,16,16,256]{3,2,1,0:T(8,128)} async-done(((f32[2,16,16,256]{3,2,1,0:T(8,128)}), f32[8,16,16,256]{3,2,1,0:T(8,128)}) %all-gather.2.cloned.1.call-update) | async-done | bytes 2097168 | tf_op jit(solution)/shard_map/all_gather | solution.py:105
  59.8 3.4 collective-permute-start.7
  69.8 53.0 %while.63 = (s32[]{:T(128)}, f32[1,16,16,256]{3,2,1,0:T(8,128)}, f32[1,16,16,256]{3,2,1,0:T(8,128)}, f32[1,16,16,256]{3,2,1,0:T(8,128)}, f32[16,16,256]{2,1,0:T(...) while((s32[]{:T(128)}, f32[1,16,16,256]{3,2,1,0:T(8,128)}, ...), condition=%wide.region_2.3_spmd.clone.clone, body=%wide.region_1.2_spmd.sunk.clone.clone.sunk | while | flops 2424835 | bytes 3637479 | solution.py:136
  70.7 5.2 %collective-permute-start = (f32[1,1,16,256]{3,2,1,0:T(8,128)S(1)}, f32[1,1,16,256]{3,2,1,0:T(8,128)S(1)}, u32[]{:S(2)}, u32[]{:S(2)}) collective-permute-start(f32[1,1,16,256]{3,2,1,0:T(8,128)S(1)} %get-tuple-element.979), channel_id=1, source_target_pairs={{0,1},{1,2},{2,3},{3,4},{4,5},{5,6},{6,7},{8,9},{9,10},{10,11},{11... | collective-permute-start | bytes 49160 | tf_op jit(solution)/shard_map/while/body/eval_jaxpr/ppermute | solution.py:23
  81.9 3.5 multiply_add_fusion.6
  94.2 3.6 multiply_add_fusion.6
  106.7 3.6 multiply_add_fusion.6
  119.1 3.6 multiply_add_fusion.6
  133.2 4.0 broadcast_multiply_fusion.5
  137.2 77.8 %while.64 = (s32[]{:T(128)}, f32[8,16,16,256]{3,2,1,0:T(8,128)}, f32[8,16,16,256]{3,2,1,0:T(8,128)}, f32[8,16,16,256]{3,2,1,0:T(8,128)}, f32[16,16,256]{2,1,0:T(...) while((s32[]{:T(128)}, f32[8,16,16,256]{3,2,1,0:T(8,128)}, ...), condition=%wide.region_4.5_spmd.clone.clone, body=%wide.region_3.4_spmd.sunk.clone.clone.sunk | while | flops 14811139 | bytes 23068904 | solution.py:136
  139.5 3.3 collective-permute-start.2
  147.0 3.2 collective-permute-done.3
  150.3 7.1 %multiply_add_fusion.7 = (f32[8,16,16,256]{3,2,1,0:T(8,128)}, f32[8,16,16,256]{3,2,1,0:T(8,128)}, f32[8,16,16,256]{3,2,1,0:T(8,128)}) fusion(f32[8,16,16,256]{3,2,1,0:T(8,128)S(1)} %copy.50, f32[]{:T(128)} %bitcast.98, f32[]{:T(128)} %bitcast.99, f32[8,16,16,256]{3,2,1,0:T(8,128)} %get-tuple-element.1066, f32[16,16,256]{2,1,0:T(8,128)S(1)} %get-tuple-element.991, ...), kind=kLoop, calls=%fused_computation.69.clone.1 | loop fusion | flops 14155776 | bytes 14417929 | tf_op jit(solution)/shard_map/while/body/eval_jaxpr/add | solution.py:133
  169.1 7.5 %multiply_add_fusion.7 = (f32[8,16,16,256]{3,2,1,0:T(8,128)}, f32[8,16,16,256]{3,2,1,0:T(8,128)}, f32[8,16,16,256]{3,2,1,0:T(8,128)}) fusion(f32[8,16,16,256]{3,2,1,0:T(8,128)S(1)} %copy.50, f32[]{:T(128)} %bitcast.98, f32[]{:T(128)} %bitcast.99, f32[8,16,16,256]{3,2,1,0:T(8,128)} %get-tuple-element.1066, f32[16,16,256]{2,1,0:T(8,128)S(1)} %get-tuple-element.991, ...), kind=kLoop, calls=%fused_computation.69.clone.1 | loop fusion | flops 14155776 | bytes 14417929 | tf_op jit(solution)/shard_map/while/body/eval_jaxpr/add | solution.py:133
  188.3 7.5 %multiply_add_fusion.7 = (f32[8,16,16,256]{3,2,1,0:T(8,128)}, f32[8,16,16,256]{3,2,1,0:T(8,128)}, f32[8,16,16,256]{3,2,1,0:T(8,128)}) fusion(f32[8,16,16,256]{3,2,1,0:T(8,128)S(1)} %copy.50, f32[]{:T(128)} %bitcast.98, f32[]{:T(128)} %bitcast.99, f32[8,16,16,256]{3,2,1,0:T(8,128)} %get-tuple-element.1066, f32[16,16,256]{2,1,0:T(8,128)S(1)} %get-tuple-element.991, ...), kind=kLoop, calls=%fused_computation.69.clone.1 | loop fusion | flops 14155776 | bytes 14417929 | tf_op jit(solution)/shard_map/while/body/eval_jaxpr/add | solution.py:133
  207.5 7.5 %multiply_add_fusion.7 = (f32[8,16,16,256]{3,2,1,0:T(8,128)}, f32[8,16,16,256]{3,2,1,0:T(8,128)}, f32[8,16,16,256]{3,2,1,0:T(8,128)}) fusion(f32[8,16,16,256]{3,2,1,0:T(8,128)S(1)} %copy.50, f32[]{:T(128)} %bitcast.98, f32[]{:T(128)} %bitcast.99, f32[8,16,16,256]{3,2,1,0:T(8,128)} %get-tuple-element.1066, f32[16,16,256]{2,1,0:T(8,128)S(1)} %get-tuple-element.991, ...), kind=kLoop, calls=%fused_computation.69.clone.1 | loop fusion | flops 14155776 | bytes 14417929 | tf_op jit(solution)/shard_map/while/body/eval_jaxpr/add | solution.py:133
  215.0 4.9 %broadcast_multiply_fusion.4 = (f32[8,16,16,256]{3,2,1,0:T(8,128)}, f32[8,16,16,256]{3,2,1,0:T(8,128)}) fusion(f32[16,16,256]{2,1,0:T(8,128)} %add.631, f32[8,16,16,256]{3,2,1,0:T(8,128)} %get-tuple-element.571, f32[8,16,16,256]{3,2,1,0:T(8,128)} %get-tuple-element.572), kind=kLoop, calls=%fused_computation.180 | loop fusion | flops 1572864 | bytes 8650752 | tf_op jit(solution)/shard_map/mul | solution.py:125
  219.9 75.9 %while.65 = (s32[]{:T(128)}, f32[8,16,16,256]{3,2,1,0:T(8,128)}, f32[8,16,16,256]{3,2,1,0:T(8,128)}, f32[8,16,16,256]{3,2,1,0:T(8,128)}, f32[16,16,256]{2,1,0:T(...) while((s32[]{:T(128)}, f32[8,16,16,256]{3,2,1,0:T(8,128)}, ...), condition=%wide.region_7.8_spmd.clone.clone, body=%wide.region_6.7_spmd.sunk.clone.clone.sunk | while | flops 14811139 | bytes 23068904 | solution.py:136
  231.6 7.0 %multiply_add_fusion.8 = (f32[8,16,16,256]{3,2,1,0:T(8,128)}, f32[8,16,16,256]{3,2,1,0:T(8,128)}, f32[8,16,16,256]{3,2,1,0:T(8,128)}) fusion(f32[8,16,16,256]{3,2,1,0:T(8,128)S(1)} %copy.51, f32[]{:T(128)} %bitcast.100, f32[]{:T(128)} %bitcast.101, f32[8,16,16,256]{3,2,1,0:T(8,128)} %get-tuple-element.1099, ...), kind=kLoop, calls=%fused_computation.110.clone.1 | loop fusion | flops 14155776 | bytes 14417929 | tf_op jit(solution)/shard_map/while/body/eval_jaxpr/add | solution.py:133
  250.3 7.3 %multiply_add_fusion.8 = (f32[8,16,16,256]{3,2,1,0:T(8,128)}, f32[8,16,16,256]{3,2,1,0:T(8,128)}, f32[8,16,16,256]{3,2,1,0:T(8,128)}) fusion(f32[8,16,16,256]{3,2,1,0:T(8,128)S(1)} %copy.51, f32[]{:T(128)} %bitcast.100, f32[]{:T(128)} %bitcast.101, f32[8,16,16,256]{3,2,1,0:T(8,128)} %get-tuple-element.1099, ...), kind=kLoop, calls=%fused_computation.110.clone.1 | loop fusion | flops 14155776 | bytes 14417929 | tf_op jit(solution)/shard_map/while/body/eval_jaxpr/add | solution.py:133
  269.4 7.3 %multiply_add_fusion.8 = (f32[8,16,16,256]{3,2,1,0:T(8,128)}, f32[8,16,16,256]{3,2,1,0:T(8,128)}, f32[8,16,16,256]{3,2,1,0:T(8,128)}) fusion(f32[8,16,16,256]{3,2,1,0:T(8,128)S(1)} %copy.51, f32[]{:T(128)} %bitcast.100, f32[]{:T(128)} %bitcast.101, f32[8,16,16,256]{3,2,1,0:T(8,128)} %get-tuple-element.1099, ...), kind=kLoop, calls=%fused_computation.110.clone.1 | loop fusion | flops 14155776 | bytes 14417929 | tf_op jit(solution)/shard_map/while/body/eval_jaxpr/add | solution.py:133
  288.5 7.3 %multiply_add_fusion.8 = (f32[8,16,16,256]{3,2,1,0:T(8,128)}, f32[8,16,16,256]{3,2,1,0:T(8,128)}, f32[8,16,16,256]{3,2,1,0:T(8,128)}) fusion(f32[8,16,16,256]{3,2,1,0:T(8,128)S(1)} %copy.51, f32[]{:T(128)} %bitcast.100, f32[]{:T(128)} %bitcast.101, f32[8,16,16,256]{3,2,1,0:T(8,128)} %get-tuple-element.1099, ...), kind=kLoop, calls=%fused_computation.110.clone.1 | loop fusion | flops 14155776 | bytes 14417929 | tf_op jit(solution)/shard_map/while/body/eval_jaxpr/add | solution.py:133
  302.9 4.8 %collective-permute-done.11 = f32[8,1,16,256]{3,2,1,0:T(8,128)S(1)} collective-permute-done((f32[8,1,16,256]{3,2,1,0:T(8,128)S(1)}, f32[8,1,16,256]{3,2,1,0:T(8,128)S(1)}, u32[]{:S(2)}, u32[]{:S(2)}) %collective-permute-start.11) | collective-permute-done | bytes 131104 | tf_op jit(solution)/shard_map/ppermute | solution.py:25
  312.7 83.9 %all-reduce.20.cloned.1.call-done = f32[8,16,16,256]{3,2,1,0:T(8,128)} async-done(((f32[8,16,16,256]{3,2,1,0:T(8,128)}), f32[8,16,16,256]{3,2,1,0:T(8,128)}) %all-reduce.20.cloned.1.call-update) | async-done | bytes 2097168 | tf_op jit(solution)/shard_map/psum | solution.py:153
  (194 shorter events, 160.8 us)
Async XLA Ops:
  6.5 47.4 %all-gather.2.cloned.1.call-start = ((), (), s32[]{:S(2)}) async-start(), calls=%async_computation | async-start | bytes 2621440 | tf_op jit(solution)/shard_map/all_gather | solution.py:105
  7.3 389.4 %all-reduce.20.cloned.1.call-start = ((), (), s32[]{:S(2)}) async-start(), calls=%async_computation.1 | async-start | bytes 4194304 | tf_op jit(solution)/shard_map/psum | solution.py:153
  56.8 10.1 %collective-permute-start.6 = (f32[9,2,16,256]{3,2,1,0:T(8,128)}, f32[9,2,16,256]{3,2,1,0:T(8,128)S(1)}, u32[]{:S(2)}, u32[]{:S(2)}) collective-permute-start(f32[9,2,16,256]{3,2,1,0:T(8,128)} %get-tuple-element.817), channel_id=1, source_target_pairs={{1,0},{2,1},{3,2},{4,3},{5,4},{6,5},{7,6},{9,8},{10,9},{11,10},{12... | collective-permute-start | bytes 884744 | tf_op jit(solution)/shard_map/ppermute | solution.py:25
  59.8 7.3 %collective-permute-start.7 = (f32[9,2,16,256]{3,2,1,0:T(8,128)}, f32[9,2,16,256]{3,2,1,0:T(8,128)S(1)}, u32[]{:S(2)}, u32[]{:S(2)}) collective-permute-start(f32[9,2,16,256]{3,2,1,0:T(8,128)} %get-tuple-element.816), channel_id=1, source_target_pairs={{0,1},{1,2},{2,3},{3,4},{4,5},{5,6},{6,7},{8,9},{9,10},{10,11},{11... | collective-permute-start | bytes 884744 | tf_op jit(solution)/shard_map/ppermute | solution.py:23
  70.7 8.4 %collective-permute-start = (f32[1,1,16,256]{3,2,1,0:T(8,128)S(1)}, f32[1,1,16,256]{3,2,1,0:T(8,128)S(1)}, u32[]{:S(2)}, u32[]{:S(2)}) collective-permute-start(f32[1,1,16,256]{3,2,1,0:T(8,128)S(1)} %get-tuple-element.979), channel_id=1, source_target_pairs={{0,1},{1,2},{2,3},{3,4},{4,5},{5,6},{6,7},{8,9},{9,10},{10,11},{11... | collective-permute-start | bytes 49160 | tf_op jit(solution)/shard_map/while/body/eval_jaxpr/ppermute | solution.py:23
  75.9 6.0 %collective-permute-start.1 = (f32[1,1,16,256]{3,2,1,0:T(8,128)S(1)}, f32[1,1,16,256]{3,2,1,0:T(8,128)S(1)}, u32[]{:S(2)}, u32[]{:S(2)}) collective-permute-start(f32[1,1,16,256]{3,2,1,0:T(8,128)S(1)} %get-tuple-element.980), channel_id=1, source_target_pairs={{1,0},{2,1},{3,2},{4,3},{5,4},{6,5},{7,6},{9,8},{10,9},{11,10},{12... | collective-permute-start | bytes 49160 | tf_op jit(solution)/shard_map/while/body/eval_jaxpr/ppermute | solution.py:25
  123.8 7.1 %collective-permute-start.8 = (f32[1,1,16,256]{3,2,1,0:T(8,128)S(1)}, f32[1,1,16,256]{3,2,1,0:T(8,128)S(1)}, u32[]{:S(2)}, u32[]{:S(2)}) collective-permute-start(f32[1,1,16,256]{3,2,1,0:T(8,128)S(1)} %get-tuple-element.831), channel_id=1, source_target_pairs={{0,1},{1,2},{2,3},{3,4},{4,5},{5,6},{6,7},{8,9},{9,10},{10,11},{11... | collective-permute-start | bytes 49160 | tf_op jit(solution)/shard_map/ppermute | solution.py:23
  139.5 7.5 %collective-permute-start.2 = (f32[8,1,16,256]{3,2,1,0:T(8,128)}, f32[8,1,16,256]{3,2,1,0:T(8,128)}, u32[]{:S(2)}, u32[]{:S(2)}) collective-permute-start(f32[8,1,16,256]{3,2,1,0:T(8,128)} %get-tuple-element.995), channel_id=1, source_target_pairs={{0,1},{1,2},{2,3},{3,4},{4,5},{5,6},{6,7},{8,9},{9,10},{10,11},{11... | collective-permute-start | bytes 393224 | tf_op jit(solution)/shard_map/while/body/eval_jaxpr/ppermute | solution.py:23
  142.8 7.5 %collective-permute-start.3 = (f32[8,1,16,256]{3,2,1,0:T(8,128)}, f32[8,1,16,256]{3,2,1,0:T(8,128)}, u32[]{:S(2)}, u32[]{:S(2)}) collective-permute-start(f32[8,1,16,256]{3,2,1,0:T(8,128)} %get-tuple-element.997), channel_id=1, source_target_pairs={{1,0},{2,1},{3,2},{4,3},{5,4},{6,5},{7,6},{9,8},{10,9},{11,10},{12... | collective-permute-start | bytes 393224 | tf_op jit(solution)/shard_map/while/body/eval_jaxpr/ppermute | solution.py:25
  159.7 6.7 %collective-permute-start.2 = (f32[8,1,16,256]{3,2,1,0:T(8,128)}, f32[8,1,16,256]{3,2,1,0:T(8,128)}, u32[]{:S(2)}, u32[]{:S(2)}) collective-permute-start(f32[8,1,16,256]{3,2,1,0:T(8,128)} %get-tuple-element.995), channel_id=1, source_target_pairs={{0,1},{1,2},{2,3},{3,4},{4,5},{5,6},{6,7},{8,9},{9,10},{10,11},{11... | collective-permute-start | bytes 393224 | tf_op jit(solution)/shard_map/while/body/eval_jaxpr/ppermute | solution.py:23
  161.6 7.5 %collective-permute-start.3 = (f32[8,1,16,256]{3,2,1,0:T(8,128)}, f32[8,1,16,256]{3,2,1,0:T(8,128)}, u32[]{:S(2)}, u32[]{:S(2)}) collective-permute-start(f32[8,1,16,256]{3,2,1,0:T(8,128)} %get-tuple-element.997), channel_id=1, source_target_pairs={{1,0},{2,1},{3,2},{4,3},{5,4},{6,5},{7,6},{9,8},{10,9},{11,10},{12... | collective-permute-start | bytes 393224 | tf_op jit(solution)/shard_map/while/body/eval_jaxpr/ppermute | solution.py:25
  178.9 6.7 %collective-permute-start.2 = (f32[8,1,16,256]{3,2,1,0:T(8,128)}, f32[8,1,16,256]{3,2,1,0:T(8,128)}, u32[]{:S(2)}, u32[]{:S(2)}) collective-permute-start(f32[8,1,16,256]{3,2,1,0:T(8,128)} %get-tuple-element.995), channel_id=1, source_target_pairs={{0,1},{1,2},{2,3},{3,4},{4,5},{5,6},{6,7},{8,9},{9,10},{10,11},{11... | collective-permute-start | bytes 393224 | tf_op jit(solution)/shard_map/while/body/eval_jaxpr/ppermute | solution.py:23
  180.8 7.5 %collective-permute-start.3 = (f32[8,1,16,256]{3,2,1,0:T(8,128)}, f32[8,1,16,256]{3,2,1,0:T(8,128)}, u32[]{:S(2)}, u32[]{:S(2)}) collective-permute-start(f32[8,1,16,256]{3,2,1,0:T(8,128)} %get-tuple-element.997), channel_id=1, source_target_pairs={{1,0},{2,1},{3,2},{4,3},{5,4},{6,5},{7,6},{9,8},{10,9},{11,10},{12... | collective-permute-start | bytes 393224 | tf_op jit(solution)/shard_map/while/body/eval_jaxpr/ppermute | solution.py:25
  198.1 6.7 %collective-permute-start.2 = (f32[8,1,16,256]{3,2,1,0:T(8,128)}, f32[8,1,16,256]{3,2,1,0:T(8,128)}, u32[]{:S(2)}, u32[]{:S(2)}) collective-permute-start(f32[8,1,16,256]{3,2,1,0:T(8,128)} %get-tuple-element.995), channel_id=1, source_target_pairs={{0,1},{1,2},{2,3},{3,4},{4,5},{5,6},{6,7},{8,9},{9,10},{10,11},{11... | collective-permute-start | bytes 393224 | tf_op jit(solution)/shard_map/while/body/eval_jaxpr/ppermute | solution.py:23
  200.0 7.5 %collective-permute-start.3 = (f32[8,1,16,256]{3,2,1,0:T(8,128)}, f32[8,1,16,256]{3,2,1,0:T(8,128)}, u32[]{:S(2)}, u32[]{:S(2)}) collective-permute-start(f32[8,1,16,256]{3,2,1,0:T(8,128)} %get-tuple-element.997), channel_id=1, source_target_pairs={{1,0},{2,1},{3,2},{4,3},{5,4},{6,5},{7,6},{9,8},{10,9},{11,10},{12... | collective-permute-start | bytes 393224 | tf_op jit(solution)/shard_map/while/body/eval_jaxpr/ppermute | solution.py:25
  222.2 6.6 %collective-permute-start.4 = (f32[8,1,16,256]{3,2,1,0:T(8,128)}, f32[8,1,16,256]{3,2,1,0:T(8,128)}, u32[]{:S(2)}, u32[]{:S(2)}) collective-permute-start(f32[8,1,16,256]{3,2,1,0:T(8,128)} %get-tuple-element.1013), channel_id=1, source_target_pairs={{0,1},{1,2},{2,3},{3,4},{4,5},{5,6},{6,7},{8,9},{9,10},{10,11},{11... | collective-permute-start | bytes 393224 | tf_op jit(solution)/shard_map/while/body/eval_jaxpr/ppermute | solution.py:23
  224.1 7.5 %collective-permute-start.5 = (f32[8,1,16,256]{3,2,1,0:T(8,128)}, f32[8,1,16,256]{3,2,1,0:T(8,128)}, u32[]{:S(2)}, u32[]{:S(2)}) collective-permute-start(f32[8,1,16,256]{3,2,1,0:T(8,128)} %get-tuple-element.1015), channel_id=1, source_target_pairs={{1,0},{2,1},{3,2},{4,3},{5,4},{6,5},{7,6},{9,8},{10,9},{11,10},{12... | collective-permute-start | bytes 393224 | tf_op jit(solution)/shard_map/while/body/eval_jaxpr/ppermute | solution.py:25
  240.9 6.6 %collective-permute-start.4 = (f32[8,1,16,256]{3,2,1,0:T(8,128)}, f32[8,1,16,256]{3,2,1,0:T(8,128)}, u32[]{:S(2)}, u32[]{:S(2)}) collective-permute-start(f32[8,1,16,256]{3,2,1,0:T(8,128)} %get-tuple-element.1013), channel_id=1, source_target_pairs={{0,1},{1,2},{2,3},{3,4},{4,5},{5,6},{6,7},{8,9},{9,10},{10,11},{11... | collective-permute-start | bytes 393224 | tf_op jit(solution)/shard_map/while/body/eval_jaxpr/ppermute | solution.py:23
  242.8 7.5 %collective-permute-start.5 = (f32[8,1,16,256]{3,2,1,0:T(8,128)}, f32[8,1,16,256]{3,2,1,0:T(8,128)}, u32[]{:S(2)}, u32[]{:S(2)}) collective-permute-start(f32[8,1,16,256]{3,2,1,0:T(8,128)} %get-tuple-element.1015), channel_id=1, source_target_pairs={{1,0},{2,1},{3,2},{4,3},{5,4},{6,5},{7,6},{9,8},{10,9},{11,10},{12... | collective-permute-start | bytes 393224 | tf_op jit(solution)/shard_map/while/body/eval_jaxpr/ppermute | solution.py:25
  260.0 6.6 %collective-permute-start.4 = (f32[8,1,16,256]{3,2,1,0:T(8,128)}, f32[8,1,16,256]{3,2,1,0:T(8,128)}, u32[]{:S(2)}, u32[]{:S(2)}) collective-permute-start(f32[8,1,16,256]{3,2,1,0:T(8,128)} %get-tuple-element.1013), channel_id=1, source_target_pairs={{0,1},{1,2},{2,3},{3,4},{4,5},{5,6},{6,7},{8,9},{9,10},{10,11},{11... | collective-permute-start | bytes 393224 | tf_op jit(solution)/shard_map/while/body/eval_jaxpr/ppermute | solution.py:23
  261.9 7.5 %collective-permute-start.5 = (f32[8,1,16,256]{3,2,1,0:T(8,128)}, f32[8,1,16,256]{3,2,1,0:T(8,128)}, u32[]{:S(2)}, u32[]{:S(2)}) collective-permute-start(f32[8,1,16,256]{3,2,1,0:T(8,128)} %get-tuple-element.1015), channel_id=1, source_target_pairs={{1,0},{2,1},{3,2},{4,3},{5,4},{6,5},{7,6},{9,8},{10,9},{11,10},{12... | collective-permute-start | bytes 393224 | tf_op jit(solution)/shard_map/while/body/eval_jaxpr/ppermute | solution.py:25
  279.1 6.6 %collective-permute-start.4 = (f32[8,1,16,256]{3,2,1,0:T(8,128)}, f32[8,1,16,256]{3,2,1,0:T(8,128)}, u32[]{:S(2)}, u32[]{:S(2)}) collective-permute-start(f32[8,1,16,256]{3,2,1,0:T(8,128)} %get-tuple-element.1013), channel_id=1, source_target_pairs={{0,1},{1,2},{2,3},{3,4},{4,5},{5,6},{6,7},{8,9},{9,10},{10,11},{11... | collective-permute-start | bytes 393224 | tf_op jit(solution)/shard_map/while/body/eval_jaxpr/ppermute | solution.py:23
  281.0 7.5 %collective-permute-start.5 = (f32[8,1,16,256]{3,2,1,0:T(8,128)}, f32[8,1,16,256]{3,2,1,0:T(8,128)}, u32[]{:S(2)}, u32[]{:S(2)}) collective-permute-start(f32[8,1,16,256]{3,2,1,0:T(8,128)} %get-tuple-element.1015), channel_id=1, source_target_pairs={{1,0},{2,1},{3,2},{4,3},{5,4},{6,5},{7,6},{9,8},{10,9},{11,10},{12... | collective-permute-start | bytes 393224 | tf_op jit(solution)/shard_map/while/body/eval_jaxpr/ppermute | solution.py:25
  300.5 7.2 %collective-permute-start.11 = (f32[8,1,16,256]{3,2,1,0:T(8,128)S(1)}, f32[8,1,16,256]{3,2,1,0:T(8,128)S(1)}, u32[]{:S(2)}, u32[]{:S(2)}) collective-permute-start(f32[8,1,16,256]{3,2,1,0:T(8,128)S(1)} %get-tuple-element.819), channel_id=1, source_target_pairs={{1,0},{2,1},{3,2},{4,3},{5,4},{6,5},{7,6},{9,8},{10,9},{11,10},{12... | collective-permute-start | bytes 393224 | tf_op jit(solution)/shard_map/ppermute | solution.py:25
  (25 other events, 137.2 us)
Sparse Core Ops, SparseCore 0:
  8.9 44.9 all-gather.1
  312.8 83.7 all-reduce.19
where the time goes:
time: 410 us; the launch traced here: 405 us
  waiting for transfers between devices  168 us (41%)
  other arithmetic  110 us (27%)
  starting transfers between devices  70.6 us (17%)
  local copies, waits for them, and re-layouts  42.8 us (10%)
  between operations  13.7 us (3%)
    psum x1, waiting for transfers between devices, shards(): total = lax.psum(partial_value, 'test')  83.9 us
    add x12, other arithmetic, sweep(): direction = keep_table[turn] * direction + push_table[turn] * residual  72.8 us
    all_gather x1, waiting for transfers between devices, shards(): columns = lax.all_gather(panel, 'test', axis=0, tiled=True)  44.8 us
    ppermute x15, waiting for transfers between devices, with_halo(): lax.ppermute(head, axis, [((i + 1) % count, i) for i in range(ends)])  37.9 us
    ppermute x15, starting transfers between devices, with_halo(): lax.ppermute(head, axis, [((i + 1) % count, i) for i in range(ends)])  35.7 us
    ppermute x15, starting transfers between devices, with_halo(): lax.ppermute(tail, axis, [(i, (i + 1) % count) for i in range(ends)])  34.8 us
    while x12, local copies, waits for them, and re-layouts  16.5 us
    dynamic_slice x24, local copies, waits for them, and re-layouts, sweep(): direction = keep_table[turn] * direction + push_table[turn] * residual  15.1 us
  transfers between devices with their start and end apart: 32, of which 17 were waited for; matrix products, arithmetic and copies ran while one was open for 8% of the time, Pallas kernels for 0%

commit v1 on v0

v1 whole, which is shorter than its diff:
```python
import math

import jax
import jax.numpy as jnp
from jax import lax
from jax.sharding import PartitionSpec as P

CHEB = 4


storage = 0.02


def with_halo(cells, axis, dim, width):
    count = lax.axis_size(axis)
    ends = count - 1
    head = lax.slice_in_dim(cells, 0, width, axis=dim)
    tail = lax.slice_in_dim(cells, cells.shape[dim] - width, cells.shape[dim], axis=dim)
    return jnp.concatenate(
        [
            lax.ppermute(tail, axis, [(i, i + 1) for i in range(ends)]),
            cells,
            lax.ppermute(head, axis, [(i + 1, i) for i in range(ends)]),
        ],
        axis=dim,
    )


def cheb_table(count):
    highest = storage + 12.0 * math.e
    theta = 0.5 * (highest + storage)
    spread = 0.5 * (highest - storage)
    sigma = theta / spread
    rho = 1.0 / sigma
    keeps = []
    pushes = []
    for turn in range(count):
        after = 1.0 / (2.0 * sigma - rho)
        keeps.append(after * rho)
        pushes.append(2.0 * after / spread)
        rho = after
    return (1.0 / theta, keeps, pushes)


def neighbours(field, back):
    axis = field.ndim - back
    widths = [(0, 0)] * field.ndim
    widths[axis] = (1, 1)
    padded = jnp.pad(field, widths)
    length = field.shape[axis]
    return (
        lax.slice_in_dim(padded, 2, length + 2, axis=axis),
        lax.slice_in_dim(padded, 0, length, axis=axis),
    )


def diffuse(weight_ext, field_ext):
    weight = weight_ext[..., 1:-1, :, :]
    field = field_ext[..., 1:-1, :, :]
    total = 0.5 * (weight + weight_ext[..., 2:, :, :]) * (field - field_ext[..., 2:, :, :])
    total = total + 0.5 * (weight + weight_ext[..., :-2, :, :]) * (
        field - field_ext[..., :-2, :, :]
    )
    for back in (2, 1):
        weight_up, weight_down = neighbours(weight, back)
        field_up, field_down = neighbours(field, back)
        total = (
            total
            + 0.5 * (weight + weight_up) * (field - field_up)
            + 0.5 * (weight + weight_down) * (field - field_down)
        )
    return total


def pairs(left_ext, right_ext):
    left = left_ext[..., 1:-1, :, :]
    right = right_ext[..., 1:-1, :, :]
    total = (left - left_ext[..., 2:, :, :]) * (right - right_ext[..., 2:, :, :])
    total = total + (left - left_ext[..., :-2, :, :]) * (right - right_ext[..., :-2, :, :])
    for back in (2, 1):
        left_up, left_down = neighbours(left, back)
        right_up, right_down = neighbours(right, back)
        total = (
            total
            + (left - left_up) * (right - right_up)
            + (left - left_down) * (right - right_down)
        )
    return total


def inner(field):
    return field[..., 1:-1, :, :]


def shards(log_perm, panel, wells, rates, recharge, gauge):
    place = lax.axis_index("cell")
    parts = lax.axis_size("cell")
    slab, rows_y, depth_z = log_perm.shape
    cols = panel.shape[0]
    first, keeps, pushes = cheb_table(CHEB)
    reach = 5
    perm = jnp.exp(log_perm)
    scaled = perm[None] * panel
    rech = lax.all_gather(recharge, "test", axis=0, tiled=True)
    wells_all = lax.all_gather(wells, "test", axis=0, tiled=True)
    rates_all = lax.all_gather(rates, "test", axis=0, tiled=True)
    tests = rech.shape[0]
    stacked = jnp.concatenate([perm[None], scaled, rech], axis=0)
    ext = with_halo(stacked, "cell", 1, reach)
    perm_ext = ext[0]
    scaled_ext = ext[1 : 1 + cols]
    rech_ext = ext[1 + cols :]
    rows_ext = slab + 2 * reach
    gx = place * slab - reach + jnp.arange(rows_ext, dtype=jnp.int32)
    mask_ext = ((gx >= 0) & (gx < parts * slab)).astype(jnp.float32)[:, None, None]
    flat = (
        gx[:, None, None] * (rows_y * depth_z)
        + jnp.arange(rows_y, dtype=jnp.int32)[None, :, None] * depth_z
        + jnp.arange(depth_z, dtype=jnp.int32)[None, None, :]
    )
    hits = wells_all[:, :, None, None, None] == flat[None, None]
    points = jnp.sum(jnp.where(hits, rates_all[:, :, None, None, None], 0.0), axis=1)
    own_hits = hits[:, :, reach : reach + slab]
    counts = jnp.sum(own_hits.astype(jnp.float32), axis=1)
    source_ext = rech_ext + points
    observe = gauge[None] + counts

    def rows_of(field, halo):
        return lax.slice_in_dim(field, reach - halo, reach + slab + halo, axis=field.ndim - 3)

    def solve(right_side, halo):
        solution = jnp.zeros_like(right_side)
        residual = right_side
        direction = right_side * first
        for turn in range(CHEB):
            weight = rows_of(perm_ext, halo)
            image = storage * inner(direction) + diffuse(weight, direction)
            solution = inner(solution) + inner(direction)
            residual = inner(residual) - image
            halo -= 1
            direction = (keeps[turn] * inner(direction) + pushes[turn] * residual) * rows_of(
                mask_ext, halo
            )
        return solution + direction, halo

    state, state_halo = solve(source_ext, reach)
    forcing = -diffuse(rows_of(scaled_ext, state_halo)[None], state[:, None])
    forcing = forcing.reshape(tests * cols, slab, rows_y, depth_z)
    forcing_ext = with_halo(forcing, "cell", 1, CHEB)
    change, _ = solve(forcing_ext, CHEB)
    weighted = (
        change.reshape(tests, cols, slab, rows_y, depth_z) * observe[:, None]
    ).reshape(tests * cols, slab, rows_y, depth_z)
    weighted_ext = with_halo(weighted, "cell", 1, CHEB + 1)
    adjoint, _ = solve(weighted_ext, CHEB + 1)
    adjoint = adjoint.reshape(tests, cols, slab + 2, rows_y, depth_z)
    contrib = jnp.sum(pairs(state[:, None], adjoint), axis=0)
    return -0.5 * perm[None] * contrib


def solution(mesh):
    return jax.shard_map(
        shards,
        mesh=mesh,
        in_specs=(
            P("cell", None, None),
            P("test", "cell", None, None),
            P("test", None),
            P("test", None),
            P("test", "cell", None, None),
            P("cell", None, None),
        ),
        out_specs=P("test", "cell", None, None),
        check_vma=False,
    )
```

time: 410 us -> 183 us (0.45)
  the two profiles are of different devices: /device:TPU:11 before, /device:TPU:1 now
where the time goes in v1:
time: 183 us
  other arithmetic  71.1 us (39%)
  waiting for transfers between devices  40.4 us (22%)
  local copies, waits for them, and re-layouts  22.4 us (12%)
  blocking collectives  17.6 us (10%)
  starting transfers between devices  16.9 us (9%)
  between operations  14.6 us (8%)
    mul x9, other arithmetic, solve(): (keeps[turn] * inner(direction) + pushes[turn] * residual) * rows_of(mask...  37.2 us
    ppermute x3, waiting for transfers between devices, with_halo(): lax.ppermute(head, axis, [(i + 1, i) for i in range(ends)])  18.5 us
    all_gather x1, waiting for transfers between devices, shards(): rech = lax.all_gather(recharge, 'test', axis=0, tiled=True)  14.4 us
    unnamed x148, local copies, waits for them, and re-layouts  12.9 us
    all_gather x1, blocking collectives, shards(): wells_all = lax.all_gather(wells, 'test', axis=0, tiled=True)  10.1 us
    ppermute x3, starting transfers between devices, with_halo(): lax.ppermute(tail, axis, [(i, i + 1) for i in range(ends)])  10.1 us
    slice x18, local copies, waits for them, and re-layouts, inner(): return field[..., 1:-1, :, :]  8.7 us
    all_gather x1, blocking collectives, shards(): rates_all = lax.all_gather(rates, 'test', axis=0, tiled=True)  7.5 us
  transfers between devices with their start and end apart: 7, of which 6 were waited for; matrix products, arithmetic and copies ran while one was open for 6% of the time, Pallas kernels for 0%

profile of v1, /device:TPU:1, one launch (start us, length us, event | category | flops | bytes accessed | tf_op | source)
XLA Modules:
  0.0 182.9 jit_solution(7672152493958785220)
XLA Ops:
  7.3 10.1 %all-gather = s32[4,1,8]{2,1,0:T(1,128)S(1)} all-gather(s32[1,1,8]{2,1,0:T(1,128)} %bitcast.73), channel_id=1, replica_groups=mesh['test'=4,'cell'=8] {'test'}, dimensions={0}, use_global_device_ids=true | all-gather | bytes 160 | tf_op jit(solution)/shard_map/all_gather | solution.py:105
  24.1 14.4 %all-gather.4.cloned.1.call-done = f32[4,16,16,256]{3,2,1,0:T(8,128)} async-done(((f32[1,16,16,256]{3,2,1,0:T(8,128)}), f32[4,16,16,256]{3,2,1,0:T(8,128)}) %all-gather.4.cloned.1.call-update) | async-done | bytes 1048592 | tf_op jit(solution)/shard_map/all_gather | solution.py:104
  39.7 4.3 %collective-permute-start = (f32[7,5,16,256]{3,2,1,0:T(8,128)S(1)}, f32[7,5,16,256]{3,2,1,0:T(8,128)S(1)}, u32[]{:S(2)}, u32[]{:S(2)}) collective-permute-start(f32[7,5,16,256]{3,2,1,0:T(8,128)S(1)} %get-tuple-element.47), channel_id=1, source_target_pairs={{0,1},{1,2},{2,3},{3,4},{4,5},{5,6},{6,7},{8,9},{9,10},{10,11},{11... | collective-permute-start | bytes 1720328 | tf_op jit(solution)/shard_map/ppermute | solution.py:21
  43.9 1.9 %collective-permute-start.1 = (f32[7,5,16,256]{3,2,1,0:T(8,128)S(1)}, f32[7,5,16,256]{3,2,1,0:T(8,128)S(1)}, u32[]{:S(2)}, u32[]{:S(2)}) collective-permute-start(f32[7,5,16,256]{3,2,1,0:T(8,128)S(1)} %get-tuple-element.48), channel_id=1, source_target_pairs={{1,0},{2,1},{3,2},{4,3},{5,4},{6,5},{7,6},{9,8},{10,9},{11,10},{12... | collective-permute-start | bytes 1720328 | tf_op jit(solution)/shard_map/ppermute | solution.py:23
  47.0 7.5 %all-gather.1 = f32[4,1,8]{2,1,0:T(1,128)S(1)} all-gather(f32[1,1,8]{2,1,0:T(1,128)S(1)} %bitcast.74), channel_id=1, replica_groups=mesh['test'=4,'cell'=8] {'test'}, dimensions={0}, use_global_device_ids=true | all-gather | bytes 160 | tf_op jit(solution)/shard_map/all_gather | solution.py:106
  60.2 2.2 %add_multiply_fusion.6 = (f32[4,24,16,256]{3,2,1,0:T(8,128)S(1)}, f32[4,24,16,256]{3,2,1,0:T(8,128)S(1)}) fusion(f32[24]{0:T(128)S(1)} %slice.712, f32[4,26,16,256]{3,2,1,0:T(8,128)S(1)} %get-tuple-element.23, f32[4,24,16,256]{3,2,1,0:T(8,128)S(1)} %slice.872, f32[24,16,256]{2,1,0:T(8,128)S(1)} %get-tuple-element.64, ...), kind=kLoop, calls=%fused_computation.276 | loop fusion | flops 9437184 | bytes 13369440 | tf_op jit(solution)/shard_map/mul | solution.py:141
  63.8 2.0 %add_multiply_fusion.7 = (f32[4,22,16,256]{3,2,1,0:T(8,128)S(1)}, f32[4,22,16,256]{3,2,1,0:T(8,128)S(1)}) fusion(f32[22]{0:T(128)S(1)} %slice.730, f32[4,24,16,256]{3,2,1,0:T(8,128)S(1)} %get-tuple-element.21, f32[4,22,16,256]{3,2,1,0:T(8,128)S(1)} %slice.879, f32[22,16,256]{2,1,0:T(8,128)S(1)} %get-tuple-element.68, ...), kind=kLoop, calls=%fused_computation.296 | loop fusion | flops 8650752 | bytes 12255320 | tf_op jit(solution)/shard_map/mul | solution.py:141
  73.4 3.9 %collective-permute-start.2 = (f32[8,4,16,256]{3,2,1,0:T(8,128)S(1)}, f32[8,4,16,256]{3,2,1,0:T(8,128)S(1)}, u32[]{:S(2)}, u32[]{:S(2)}) collective-permute-start(f32[8,4,16,256]{3,2,1,0:T(8,128)S(1)} %get-tuple-element.43), channel_id=1, source_target_pairs={{0,1},{1,2},{2,3},{3,4},{4,5},{5,6},{6,7},{8,9},{9,10},{10,11},{11... | collective-permute-start | bytes 1572872 | tf_op jit(solution)/shard_map/ppermute | solution.py:21
  77.4 2.1 %collective-permute-start.3 = (f32[8,4,16,256]{3,2,1,0:T(8,128)S(1)}, f32[8,4,16,256]{3,2,1,0:T(8,128)S(1)}, u32[]{:S(2)}, u32[]{:S(2)}) collective-permute-start(f32[8,4,16,256]{3,2,1,0:T(8,128)S(1)} %get-tuple-element.44), channel_id=1, source_target_pairs={{1,0},{2,1},{3,2},{4,3},{5,4},{6,5},{7,6},{9,8},{10,9},{11,10},{12... | collective-permute-start | bytes 1572872 | tf_op jit(solution)/shard_map/ppermute | solution.py:23
  81.5 2.0 %collective-permute-done.2 = f32[8,4,16,256]{3,2,1,0:T(8,128)S(1)} collective-permute-done((f32[8,4,16,256]{3,2,1,0:T(8,128)S(1)}, f32[8,4,16,256]{3,2,1,0:T(8,128)S(1)}, u32[]{:S(2)}, u32[]{:S(2)}) %collective-permute-start.2) | collective-permute-done | bytes 524320 | tf_op jit(solution)/shard_map/ppermute | solution.py:21
  83.5 8.1 %collective-permute-done.3 = f32[8,4,16,256]{3,2,1,0:T(8,128)S(1)} collective-permute-done((f32[8,4,16,256]{3,2,1,0:T(8,128)S(1)}, f32[8,4,16,256]{3,2,1,0:T(8,128)S(1)}, u32[]{:S(2)}, u32[]{:S(2)}) %collective-permute-start.3) | collective-permute-done | bytes 524320 | tf_op jit(solution)/shard_map/ppermute | solution.py:23
  95.1 5.1 %add_multiply_fusion.2 = (f32[8,22,16,256]{3,2,1,0:T(8,128)S(1)}, f32[8,22,16,256]{3,2,1,0:T(8,128)S(1)}) fusion(f32[22]{0:T(128)S(1)} %slice.730, f32[8,24,16,256]{3,2,1,0:T(8,128)S(1)} %get-tuple-element.30, f32[8,22,16,256]{3,2,1,0:T(8,128)S(1)} %slice.913, f32[22,16,256]{2,1,0:T(8,128)S(1)} %get-tuple-element.68, f32[22,16,256]{2,1,0:T(8,128)} %copy-done.19, ...), kind=kLoop, calls=%fused_computation.101 | loop fusion | flops 17301504 | bytes 22347864 | tf_op jit(solution)/shard_map/mul | solution.py:141
  101.9 3.5 %add_multiply_fusion.4 = (f32[8,20,16,256]{3,2,1,0:T(8,128)S(1)}, f32[8,20,16,256]{3,2,1,0:T(8,128)S(1)}) fusion(f32[20]{0:T(128)S(1)} %slice.748, f32[8,22,16,256]{3,2,1,0:T(8,128)S(1)} %get-tuple-element.15, f32[8,20,16,256]{3,2,1,0:T(8,128)S(1)} %slice.917, f32[20,16,256]{2,1,0:T(8,128)S(1)} %copy-done.26, f32[20,16,256]{2,1,0:T(8,128)S(1)} %copy-done.32, ...), kind=kLoop, calls=%fused_computation.141 | loop fusion | flops 15728640 | bytes 20316240 | tf_op jit(solution)/shard_map/mul | solution.py:141
  106.9 3.2 %add_multiply_fusion.5 = (f32[8,18,16,256]{3,2,1,0:T(8,128)S(1)}, f32[8,18,16,256]{3,2,1,0:T(8,128)S(1)}) fusion(f32[18]{0:T(128)S(1)} %slice.765, f32[8,20,16,256]{3,2,1,0:T(8,128)S(1)} %get-tuple-element.13, f32[8,18,16,256]{3,2,1,0:T(8,128)S(1)} %slice.923, f32[18,16,256]{2,1,0:T(8,128)S(1)} %copy-done.50, f32[18,16,256]{2,1,0:T(8,128)S(1)} %copy-done.55, ...), kind=kLoop, calls=%fused_computation.195 | loop fusion | flops 14155776 | bytes 18284616 | tf_op jit(solution)/shard_map/mul | solution.py:141
  112.2 3.4 %fusion.136 = f32[8,16,16,256]{3,2,1,0:T(8,128)S(1)} fusion(f32[8,16,16,256]{3,2,1,0:T(8,128)S(1)} %slice.930, f32[8,18,16,256]{3,2,1,0:T(8,128)S(1)} %get-tuple-element.11, f32[8,18,16,256]{3,2,1,0:T(8,128)S(1)} %get-tuple-element.12, f32[8,18,16,256]{3,2,1,0:T(8,128)S(1)} %slice.923, f32[8,18,16,256]{3,2,1,0:T(8,128)S(1)} %slice.919, ...), kind=kLoop, calls=%fused_computation.212 | loop fusion | flops 15204352 | bytes 19398720 | tf_op jit(solution)/shard_map/mul | solution.py:152
  117.7 2.7 %collective-permute-start.5 = (f32[8,5,16,256]{3,2,1,0:T(8,128)S(1)}, f32[8,5,16,256]{3,2,1,0:T(8,128)S(1)}, u32[]{:S(2)}, u32[]{:S(2)}) collective-permute-start(f32[8,5,16,256]{3,2,1,0:T(8,128)S(1)} %get-tuple-element.42), channel_id=1, source_target_pairs={{1,0},{2,1},{3,2},{4,3},{5,4},{6,5},{7,6},{9,8},{10,9},{11,10},{12... | collective-permute-start | bytes 1966088 | tf_op jit(solution)/shard_map/ppermute | solution.py:23
  120.4 4.8 %collective-permute-done.4 = f32[8,5,16,256]{3,2,1,0:T(8,128)S(1)} collective-permute-done((f32[8,5,16,256]{3,2,1,0:T(8,128)S(1)}, f32[8,5,16,256]{3,2,1,0:T(8,128)S(1)}, u32[]{:S(2)}, u32[]{:S(2)}) %collective-permute-start.4) | collective-permute-done | bytes 655392 | tf_op jit(solution)/shard_map/ppermute | solution.py:21
  125.2 8.5 %collective-permute-done.5 = f32[8,5,16,256]{3,2,1,0:T(8,128)S(1)} collective-permute-done((f32[8,5,16,256]{3,2,1,0:T(8,128)S(1)}, f32[8,5,16,256]{3,2,1,0:T(8,128)S(1)}, u32[]{:S(2)}, u32[]{:S(2)}) %collective-permute-start.5) | collective-permute-done | bytes 655392 | tf_op jit(solution)/shard_map/ppermute | solution.py:23
  136.6 2.0 %slice.938 = f32[8,24,16,256]{3,2,1,0:T(8,128)} slice(f32[8,26,16,256]{3,2,1,0:T(8,128)S(1)} %get-tuple-element.28), slice={[0:8], [1:25], [0:16], [0:256]} | slice | bytes 6291456 | tf_op jit(solution)/shard_map/slice | solution.py:92
  138.6 10.1 %add_multiply_fusion = (f32[8,24,16,256]{3,2,1,0:T(8,128)S(1)}, f32[8,24,16,256]{3,2,1,0:T(8,128)}) fusion(f32[24]{0:T(128)S(1)} %slice.712, f32[8,26,16,256]{3,2,1,0:T(8,128)S(1)} %get-tuple-element.28, f32[8,24,16,256]{3,2,1,0:T(8,128)} %slice.938, f32[24,16,256]{2,1,0:T(8,128)} %copy-done.62, f32[24,16,256]{2,1,0:T(8,128)} %copy-done.64, ...), kind=kLoop, calls=%fused_computation.60 | loop fusion | flops 18874368 | bytes 24379488 | tf_op jit(solution)/shard_map/mul | solution.py:141
  150.9 6.0 %add_multiply_fusion.1 = (f32[8,22,16,256]{3,2,1,0:T(8,128)S(1)}, f32[8,22,16,256]{3,2,1,0:T(8,128)}) fusion(f32[22]{0:T(128)S(1)} %slice.730, f32[8,24,16,256]{3,2,1,0:T(8,128)S(1)} %get-tuple-element.9, f32[8,22,16,256]{3,2,1,0:T(8,128)S(1)} %slice.942, f32[22,16,256]{2,1,0:T(8,128)S(1)} %get-tuple-element.68, f32[22,16,256]{2,1,0:T(8,128)} %copy-done.19, ...), kind=kLoop, calls=%fused_computation.100 | loop fusion | flops 17301504 | bytes 22347864 | tf_op jit(solution)/shard_map/mul | solution.py:141
  159.2 3.3 %add_multiply_fusion.3 = (f32[8,20,16,256]{3,2,1,0:T(8,128)S(1)}, f32[8,20,16,256]{3,2,1,0:T(8,128)S(1)}) fusion(f32[20]{0:T(128)S(1)} %slice.748, f32[8,22,16,256]{3,2,1,0:T(8,128)S(1)} %get-tuple-element.7, f32[8,20,16,256]{3,2,1,0:T(8,128)S(1)} %slice.948, f32[20,16,256]{2,1,0:T(8,128)S(1)} %copy-done.27, f32[20,16,256]{2,1,0:T(8,128)S(1)} %copy-done.33, ...), kind=kLoop, calls=%fused_computation.140 | loop fusion | flops 15728640 | bytes 20316240 | tf_op jit(solution)/shard_map/mul | solution.py:141
  164.5 4.7 %fusion.110 = f32[8,18,16,256]{3,2,1,0:T(8,128)S(1)} fusion(f32[8,18,16,256]{3,2,1,0:T(8,128)S(1)} %slice.955, f32[8,20,16,256]{3,2,1,0:T(8,128)S(1)} %get-tuple-element.5, f32[8,20,16,256]{3,2,1,0:T(8,128)S(1)} %get-tuple-element.6, f32[8,20,16,256]{3,2,1,0:T(8,128)S(1)} %slice.948, f32[8,20,16,256]{3,2,1,0:T(8,128)S(1)} %slice.944, ...), kind=kLoop, calls=%fused_computation.175 | loop fusion | flops 16515072 | bytes 20643912 | tf_op jit(solution)/shard_map/add | solution.py:144
  171.4 3.8 %fusion.149 = f32[2,16,16,256]{3,2,1,0:T(8,128)S(1)} fusion(f32[4,2,16,16,256]{4,3,2,1,0:T(8,128)S(1)} %slice.959, f32[4,2,18,16,256]{4,3,2,1,0:T(8,128)S(1)} %bitcast.67, f32[4,16,16,256]{3,2,1,0:T(8,128)S(1)} %copy-done.9, f32[4,16,16,256]{3,2,1,0:T(8,128)S(1)} %copy-done.7, f32[4,16,16,256]{3,2,1,0:T(8,128)S(1)} %copy-done.11, ...), kind=kLoop, calls=%fused_computation.225 | loop fusion | flops 9306112 | bytes 13107200 | tf_op jit(solution)/shard_map/reduce_sum | solution.py:157
  (213 shorter events, 48.8 us)
Async XLA Ops:
  6.5 32.0 %all-gather.4.cloned.1.call-start = ((), (), s32[]{:S(2)}) async-start(), calls=%async_computation | async-start | bytes 1310720 | tf_op jit(solution)/shard_map/all_gather | solution.py:104
  24.1 22.9 %copy-start.73 = (f32[1,8]{1,0:T(1,128)S(1)}, f32[1,8]{1,0:T(1,128)}, u32[]{:S(2)}) copy-start(f32[1,8]{1,0:T(1,128)} %param.9) | copy-start | bytes 100
  39.7 18.7 %copy-start = (f32[4,16,16,256]{3,2,1,0:T(8,128)S(1)}, f32[4,16,16,256]{3,2,1,0:T(8,128)}, u32[]{:S(2)}) copy-start(f32[4,16,16,256]{3,2,1,0:T(8,128)} %all-gather.4.cloned.1.call-done) | copy-start | bytes 3145732
  39.7 16.8 %collective-permute-start = (f32[7,5,16,256]{3,2,1,0:T(8,128)S(1)}, f32[7,5,16,256]{3,2,1,0:T(8,128)S(1)}, u32[]{:S(2)}, u32[]{:S(2)}) collective-permute-start(f32[7,5,16,256]{3,2,1,0:T(8,128)S(1)} %get-tuple-element.47), channel_id=1, source_target_pairs={{0,1},{1,2},{2,3},{3,4},{4,5},{5,6},{6,7},{8,9},{9,10},{10,11},{11... | collective-permute-start | bytes 1720328 | tf_op jit(solution)/shard_map/ppermute | solution.py:21
  43.9 14.4 %collective-permute-start.1 = (f32[7,5,16,256]{3,2,1,0:T(8,128)S(1)}, f32[7,5,16,256]{3,2,1,0:T(8,128)S(1)}, u32[]{:S(2)}, u32[]{:S(2)}) collective-permute-start(f32[7,5,16,256]{3,2,1,0:T(8,128)S(1)} %get-tuple-element.48), channel_id=1, source_target_pairs={{1,0},{2,1},{3,2},{4,3},{5,4},{6,5},{7,6},{9,8},{10,9},{11,10},{12... | collective-permute-start | bytes 1720328 | tf_op jit(solution)/shard_map/ppermute | solution.py:23
  58.8 7.1 %copy-start.34 = (f32[20,16,256]{2,1,0:T(8,128)}, f32[20,16,256]{2,1,0:T(8,128)S(1)}, u32[]{:S(2)}) copy-start(f32[20,16,256]{2,1,0:T(8,128)S(1)} %get-tuple-element.32) | copy-start | bytes 983044
  58.8 7.1 %copy-start.37 = (f32[20,16,256]{2,1,0:T(8,128)}, f32[20,16,256]{2,1,0:T(8,128)S(1)}, u32[]{:S(2)}) copy-start(f32[20,16,256]{2,1,0:T(8,128)S(1)} %get-tuple-element.33) | copy-start | bytes 983044
  58.9 4.8 %copy-start.20 = (f32[22,16,256]{2,1,0:T(8,128)}, f32[22,16,256]{2,1,0:T(8,128)S(1)}, u32[]{:S(2)}) copy-start(f32[22,16,256]{2,1,0:T(8,128)S(1)} %get-tuple-element.35) | copy-start | bytes 1081348
  58.9 4.8 %copy-start.21 = (f32[22,16,256]{2,1,0:T(8,128)}, f32[22,16,256]{2,1,0:T(8,128)S(1)}, u32[]{:S(2)}) copy-start(f32[22,16,256]{2,1,0:T(8,128)S(1)} %get-tuple-element.36) | copy-start | bytes 1081348
  62.7 5.1 %copy-start.40 = (f32[18,16,256]{2,1,0:T(8,128)}, f32[18,16,256]{2,1,0:T(8,128)S(1)}, u32[]{:S(2)}) copy-start(f32[18,16,256]{2,1,0:T(8,128)S(1)} %get-tuple-element.25) | copy-start | bytes 884740
  62.8 5.1 %copy-start.43 = (f32[18,16,256]{2,1,0:T(8,128)}, f32[18,16,256]{2,1,0:T(8,128)S(1)}, u32[]{:S(2)}) copy-start(f32[18,16,256]{2,1,0:T(8,128)S(1)} %get-tuple-element.26) | copy-start | bytes 884740
  63.0 4.9 %copy-start.46 = (f32[18,16,256]{2,1,0:T(8,128)}, f32[18,16,256]{2,1,0:T(8,128)S(1)}, u32[]{:S(2)}) copy-start(f32[18,16,256]{2,1,0:T(8,128)S(1)} %get-tuple-element.75) | copy-start | bytes 884740
  63.0 4.9 %copy-start.49 = (f32[18,16,256]{2,1,0:T(8,128)}, f32[18,16,256]{2,1,0:T(8,128)S(1)}, u32[]{:S(2)}) copy-start(f32[18,16,256]{2,1,0:T(8,128)S(1)} %get-tuple-element.76) | copy-start | bytes 884740
  63.0 4.9 %copy-start.52 = (f32[18,16,256]{2,1,0:T(8,128)}, f32[18,16,256]{2,1,0:T(8,128)S(1)}, u32[]{:S(2)}) copy-start(f32[18,16,256]{2,1,0:T(8,128)S(1)} %get-tuple-element.77) | copy-start | bytes 884740
  63.0 4.9 %copy-start.54 = (f32[18,16,256]{2,1,0:T(8,128)}, f32[18,16,256]{2,1,0:T(8,128)S(1)}, u32[]{:S(2)}) copy-start(f32[18,16,256]{2,1,0:T(8,128)S(1)} %get-tuple-element.78) | copy-start | bytes 884740
  71.4 8.1 %copy-start.72 = (f32[16,16,256]{2,1,0:T(8,128)S(1)}, f32[16,16,256]{2,1,0:T(8,128)}, u32[]{:S(2)}) copy-start(f32[16,16,256]{2,1,0:T(8,128)} %param.11) | copy-start | bytes 786436
  73.3 6.2 %copy-start.56 = (f32[4,16,16,256]{3,2,1,0:T(8,128)S(1)}, f32[4,16,16,256]{3,2,1,0:T(8,128)}, u32[]{:S(2)}) copy-start(f32[4,16,16,256]{3,2,1,0:T(8,128)} %convert_reduce_fusion) | copy-start | bytes 3145732
  73.4 10.0 %collective-permute-start.2 = (f32[8,4,16,256]{3,2,1,0:T(8,128)S(1)}, f32[8,4,16,256]{3,2,1,0:T(8,128)S(1)}, u32[]{:S(2)}, u32[]{:S(2)}) collective-permute-start(f32[8,4,16,256]{3,2,1,0:T(8,128)S(1)} %get-tuple-element.43), channel_id=1, source_target_pairs={{0,1},{1,2},{2,3},{3,4},{4,5},{5,6},{6,7},{8,9},{9,10},{10,11},{11... | collective-permute-start | bytes 1572872 | tf_op jit(solution)/shard_map/ppermute | solution.py:21
  77.4 14.2 %collective-permute-start.3 = (f32[8,4,16,256]{3,2,1,0:T(8,128)S(1)}, f32[8,4,16,256]{3,2,1,0:T(8,128)S(1)}, u32[]{:S(2)}, u32[]{:S(2)}) collective-permute-start(f32[8,4,16,256]{3,2,1,0:T(8,128)S(1)} %get-tuple-element.44), channel_id=1, source_target_pairs={{1,0},{2,1},{3,2},{4,3},{5,4},{6,5},{7,6},{9,8},{10,9},{11,10},{12... | collective-permute-start | bytes 1572872 | tf_op jit(solution)/shard_map/ppermute | solution.py:23
  106.9 3.6 %copy-start.70 = (f32[16,16,256]{2,1,0:T(8,128)S(1)}, f32[16,16,256]{2,1,0:T(8,128)}, u32[]{:S(2)}) copy-start(f32[16,16,256]{2,1,0:T(8,128)} %get-tuple-element.46) | copy-start | bytes 786436
  115.8 9.4 %collective-permute-start.4 = (f32[8,5,16,256]{3,2,1,0:T(8,128)S(1)}, f32[8,5,16,256]{3,2,1,0:T(8,128)S(1)}, u32[]{:S(2)}, u32[]{:S(2)}) collective-permute-start(f32[8,5,16,256]{3,2,1,0:T(8,128)S(1)} %get-tuple-element.41), channel_id=1, source_target_pairs={{0,1},{1,2},{2,3},{3,4},{4,5},{5,6},{6,7},{8,9},{9,10},{10,11},{11... | collective-permute-start | bytes 1966088 | tf_op jit(solution)/shard_map/ppermute | solution.py:21
  117.7 16.0 %collective-permute-start.5 = (f32[8,5,16,256]{3,2,1,0:T(8,128)S(1)}, f32[8,5,16,256]{3,2,1,0:T(8,128)S(1)}, u32[]{:S(2)}, u32[]{:S(2)}) collective-permute-start(f32[8,5,16,256]{3,2,1,0:T(8,128)S(1)} %get-tuple-element.42), channel_id=1, source_target_pairs={{1,0},{2,1},{3,2},{4,3},{5,4},{6,5},{7,6},{9,8},{10,9},{11,10},{12... | collective-permute-start | bytes 1966088 | tf_op jit(solution)/shard_map/ppermute | solution.py:23
  164.5 4.9 %copy-start.13 = (f32[4,16,16,256]{3,2,1,0:T(8,128)S(1)}, f32[4,16,16,256]{3,2,1,0:T(8,128)}, u32[]{:S(2)}) copy-start(f32[4,16,16,256]{3,2,1,0:T(8,128)} %copy-done.12) | copy-start | bytes 3145732
  171.4 3.8 %copy-start.71 = (f32[16,16,256]{2,1,0:T(8,128)S(1)}, f32[16,16,256]{2,1,0:T(8,128)}, u32[]{:S(2)}) copy-start(f32[16,16,256]{2,1,0:T(8,128)} %get-tuple-element.79) | copy-start | bytes 786436
  (57 other events, 103.0 us)
Sparse Core Ops, SparseCore 0:
  8.9 29.5 all-gather.3

commit v2 on v1

--- a/solution.py
+++ b/solution.py
@@ -101,10 +101,16 @@
     reach = 5
     perm = jnp.exp(log_perm)
     scaled = perm[None] * panel
-    rech = lax.all_gather(recharge, "test", axis=0, tiled=True)
-    wells_all = lax.all_gather(wells, "test", axis=0, tiled=True)
-    rates_all = lax.all_gather(rates, "test", axis=0, tiled=True)
-    tests = rech.shape[0]
+    tests_here, well_count = wells.shape
+    cells = slab * rows_y * depth_z
+    packed = jnp.concatenate(
+        [recharge.reshape(tests_here, cells), wells.astype(jnp.float32), rates], axis=1
+    )
+    packed = lax.all_gather(packed, "test", axis=0, tiled=True)
+    tests = packed.shape[0]
+    rech = packed[:, :cells].reshape(tests, slab, rows_y, depth_z)
+    wells_all = packed[:, cells : cells + well_count].astype(jnp.int32)
+    rates_all = packed[:, cells + well_count :]
     stacked = jnp.concatenate([perm[None], scaled, rech], axis=0)
     ext = with_halo(stacked, "cell", 1, reach)
     perm_ext = ext[0]

time: 183 us -> 182 us (level)
  blocking collectives: 17.6 us -> 0 us
  waiting for transfers between devices: 40.4 us -> 56 us
  local copies, waits for them, and re-layouts: 22.4 us -> 27.1 us
  starting transfers between devices: 16.9 us -> 14.8 us
  other arithmetic: 71.1 us -> 69.1 us
    all_gather x2 -> x0, blocking collectives: 17.6 us -> none  [the longest x1 10.1 us: shards(): wells_all = lax.all_gather(wells, 'test', axis=0, tiled=True)]
    all_gather x1, waiting for transfers between devices: 14.4 us -> 26.2 us  [shards(): packed = lax.all_gather(packed, 'test', axis=0, tiled=True)]
    ppermute x3, waiting for transfers between devices: 18.5 us -> 22.6 us  [with_halo(): lax.ppermute(head, axis, [(i + 1, i) for i in range(ends)])]
    unnamed x148 -> x151, local copies, waits for them, and re-layouts: 12.9 us -> 16.7 us
    ppermute x3, starting transfers between devices: 10.1 us -> 7.98 us  [with_halo(): lax.ppermute(tail, axis, [(i, i + 1) for i in range(ends)])]
  transfers between devices with their start and end apart: 7 -> 7, of which waited for: 6 -> 7; matrix products, arithmetic and copies ran while one was open for 6% -> 5% of each run, Pallas kernels for 0% -> 0%
where the time goes in v2:
time: 182 us
  other arithmetic  69.1 us (38%)
  waiting for transfers between devices  56 us (31%)
  local copies, waits for them, and re-layouts  27.1 us (15%)
  starting transfers between devices  14.8 us (8%)
  between operations  14.6 us (8%)
    mul x9, other arithmetic, solve(): (keeps[turn] * inner(direction) + pushes[turn] * residual) * rows_of(mask...  37.5 us
    all_gather x1, waiting for transfers between devices, shards(): packed = lax.all_gather(packed, 'test', axis=0, tiled=True)  26.2 us
    ppermute x3, waiting for transfers between devices, with_halo(): lax.ppermute(head, axis, [(i + 1, i) for i in range(ends)])  22.6 us
    unnamed x151, local copies, waits for them, and re-layouts  16.7 us
    slice x18, local copies, waits for them, and re-layouts, inner(): return field[..., 1:-1, :, :]  8.7 us
    ppermute x3, starting transfers between devices, with_halo(): lax.ppermute(tail, axis, [(i, i + 1) for i in range(ends)])  7.98 us
    ppermute x3, waiting for transfers between devices, with_halo(): lax.ppermute(tail, axis, [(i, i + 1) for i in range(ends)])  7.21 us
    ppermute x3, starting transfers between devices, with_halo(): lax.ppermute(head, axis, [(i + 1, i) for i in range(ends)])  6.8 us
  transfers between devices with their start and end apart: 7, of which 7 were waited for; matrix products, arithmetic and copies ran while one was open for 5% of the time, Pallas kernels for 0%

profile of v2, /device:TPU:1, one launch (start us, length us, event | category | flops | bytes accessed | tf_op | source)
XLA Modules:
  0.0 181.6 jit_solution(2463317136255908231)
XLA Ops:
  13.8 26.2 %all-gather.3.cloned.1.call-done = f32[4,1,65552]{2,1,0:T(1,128)} async-done(((f32[1,1,65552]{2,1,0:T(1,128)}), f32[4,1,65552]{2,1,0:T(1,128)}) %all-gather.3.cloned.1.call-update) | async-done | bytes 1048848 | tf_op jit(solution)/shard_map/all_gather | solution.py:109
  42.0 4.1 %collective-permute-start = (f32[7,5,16,256]{3,2,1,0:T(8,128)S(1)}, f32[7,5,16,256]{3,2,1,0:T(8,128)S(1)}, u32[]{:S(2)}, u32[]{:S(2)}) collective-permute-start(f32[7,5,16,256]{3,2,1,0:T(8,128)S(1)} %get-tuple-element.47), channel_id=1, source_target_pairs={{0,1},{1,2},{2,3},{3,4},{4,5},{5,6},{6,7},{8,9},{9,10},{10,11},{11... | collective-permute-start | bytes 1720328 | tf_op jit(solution)/shard_map/ppermute | solution.py:21
  46.1 1.9 %collective-permute-start.1 = (f32[7,5,16,256]{3,2,1,0:T(8,128)S(1)}, f32[7,5,16,256]{3,2,1,0:T(8,128)S(1)}, u32[]{:S(2)}, u32[]{:S(2)}) collective-permute-start(f32[7,5,16,256]{3,2,1,0:T(8,128)S(1)} %get-tuple-element.48), channel_id=1, source_target_pairs={{1,0},{2,1},{3,2},{4,3},{5,4},{6,5},{7,6},{9,8},{10,9},{11,10},{12... | collective-permute-start | bytes 1720328 | tf_op jit(solution)/shard_map/ppermute | solution.py:23
  52.7 7.8 %collective-permute-done.1 = f32[7,5,16,256]{3,2,1,0:T(8,128)S(1)} collective-permute-done((f32[7,5,16,256]{3,2,1,0:T(8,128)S(1)}, f32[7,5,16,256]{3,2,1,0:T(8,128)S(1)}, u32[]{:S(2)}, u32[]{:S(2)}) %collective-permute-start.1) | collective-permute-done | bytes 573472 | tf_op jit(solution)/shard_map/ppermute | solution.py:23
  62.4 2.3 %add_multiply_fusion.6 = (f32[4,24,16,256]{3,2,1,0:T(8,128)S(1)}, f32[4,24,16,256]{3,2,1,0:T(8,128)S(1)}) fusion(f32[24]{0:T(128)S(1)} %slice.724, f32[4,26,16,256]{3,2,1,0:T(8,128)S(1)} %get-tuple-element.23, f32[4,24,16,256]{3,2,1,0:T(8,128)S(1)} %slice.887, f32[24,16,256]{2,1,0:T(8,128)S(1)} %get-tuple-element.66, ...), kind=kLoop, calls=%fused_computation.276 | loop fusion | flops 9437184 | bytes 13369440 | tf_op jit(solution)/shard_map/mul | solution.py:147
  66.0 2.0 %add_multiply_fusion.7 = (f32[4,22,16,256]{3,2,1,0:T(8,128)S(1)}, f32[4,22,16,256]{3,2,1,0:T(8,128)S(1)}) fusion(f32[22]{0:T(128)S(1)} %slice.742, f32[4,24,16,256]{3,2,1,0:T(8,128)S(1)} %get-tuple-element.21, f32[4,22,16,256]{3,2,1,0:T(8,128)S(1)} %slice.894, f32[22,16,256]{2,1,0:T(8,128)S(1)} %get-tuple-element.70, ...), kind=kLoop, calls=%fused_computation.296 | loop fusion | flops 8650752 | bytes 12255320 | tf_op jit(solution)/shard_map/mul | solution.py:147
  70.2 1.9 %fusion.226 = f32[4,1,18,16,256]{4,3,2,0,1:T(8,128)S(1)} fusion(f32[4,18,16,256]{3,2,1,0:T(8,128)S(1)} %slice.913, f32[4,20,16,256]{3,2,1,0:T(8,128)S(1)} %get-tuple-element.17, f32[4,20,16,256]{3,2,1,0:T(8,128)S(1)} %get-tuple-element.18, f32[4,20,16,256]{3,2,1,0:T(8,128)S(1)} %slice.903, f32[4,20,16,256]{3,2,1,0:T(8,128)S(1)} %slice.896, ...), kind=kLoop, calls=%fused_computation.329 | loop fusion | flops 8257536 | bytes 11206728 | tf_op jit(solution)/shard_map/broadcast_in_dim | solution.py:163
  75.7 1.9 %collective-permute-start.2 = (f32[8,4,16,256]{3,2,1,0:T(8,128)S(1)}, f32[8,4,16,256]{3,2,1,0:T(8,128)S(1)}, u32[]{:S(2)}, u32[]{:S(2)}) collective-permute-start(f32[8,4,16,256]{3,2,1,0:T(8,128)S(1)} %get-tuple-element.43), channel_id=1, source_target_pairs={{0,1},{1,2},{2,3},{3,4},{4,5},{5,6},{6,7},{8,9},{9,10},{10,11},{11... | collective-permute-start | bytes 1572872 | tf_op jit(solution)/shard_map/ppermute | solution.py:21
  77.6 2.4 %collective-permute-start.3 = (f32[8,4,16,256]{3,2,1,0:T(8,128)S(1)}, f32[8,4,16,256]{3,2,1,0:T(8,128)S(1)}, u32[]{:S(2)}, u32[]{:S(2)}) collective-permute-start(f32[8,4,16,256]{3,2,1,0:T(8,128)S(1)} %get-tuple-element.44), channel_id=1, source_target_pairs={{1,0},{2,1},{3,2},{4,3},{5,4},{6,5},{7,6},{9,8},{10,9},{11,10},{12... | collective-permute-start | bytes 1572872 | tf_op jit(solution)/shard_map/ppermute | solution.py:23
  83.7 7.2 %collective-permute-done.3 = f32[8,4,16,256]{3,2,1,0:T(8,128)S(1)} collective-permute-done((f32[8,4,16,256]{3,2,1,0:T(8,128)S(1)}, f32[8,4,16,256]{3,2,1,0:T(8,128)S(1)}, u32[]{:S(2)}, u32[]{:S(2)}) %collective-permute-start.3) | collective-permute-done | bytes 524320 | tf_op jit(solution)/shard_map/ppermute | solution.py:23
  94.5 5.1 %add_multiply_fusion.2 = (f32[8,22,16,256]{3,2,1,0:T(8,128)S(1)}, f32[8,22,16,256]{3,2,1,0:T(8,128)S(1)}) fusion(f32[22]{0:T(128)S(1)} %slice.742, f32[8,24,16,256]{3,2,1,0:T(8,128)S(1)} %get-tuple-element.30, f32[8,22,16,256]{3,2,1,0:T(8,128)S(1)} %slice.928, f32[22,16,256]{2,1,0:T(8,128)S(1)} %get-tuple-element.70, f32[22,16,256]{2,1,0:T(8,128)} %copy-done.18, ...), kind=kLoop, calls=%fused_computation.101 | loop fusion | flops 17301504 | bytes 22347864 | tf_op jit(solution)/shard_map/mul | solution.py:147
  101.3 3.5 %add_multiply_fusion.4 = (f32[8,20,16,256]{3,2,1,0:T(8,128)S(1)}, f32[8,20,16,256]{3,2,1,0:T(8,128)S(1)}) fusion(f32[20]{0:T(128)S(1)} %slice.760, f32[8,22,16,256]{3,2,1,0:T(8,128)S(1)} %get-tuple-element.15, f32[8,20,16,256]{3,2,1,0:T(8,128)S(1)} %slice.932, f32[20,16,256]{2,1,0:T(8,128)S(1)} %copy-done.25, f32[20,16,256]{2,1,0:T(8,128)S(1)} %copy-done.31, ...), kind=kLoop, calls=%fused_computation.141 | loop fusion | flops 15728640 | bytes 20316240 | tf_op jit(solution)/shard_map/mul | solution.py:147
  106.2 3.2 %add_multiply_fusion.5 = (f32[8,18,16,256]{3,2,1,0:T(8,128)S(1)}, f32[8,18,16,256]{3,2,1,0:T(8,128)S(1)}) fusion(f32[18]{0:T(128)S(1)} %slice.777, f32[8,20,16,256]{3,2,1,0:T(8,128)S(1)} %get-tuple-element.13, f32[8,18,16,256]{3,2,1,0:T(8,128)S(1)} %slice.938, f32[18,16,256]{2,1,0:T(8,128)S(1)} %copy-done.49, f32[18,16,256]{2,1,0:T(8,128)S(1)} %copy-done.54, ...), kind=kLoop, calls=%fused_computation.195 | loop fusion | flops 14155776 | bytes 18284616 | tf_op jit(solution)/shard_map/mul | solution.py:147
  111.6 3.4 %fusion.136 = f32[8,16,16,256]{3,2,1,0:T(8,128)S(1)} fusion(f32[8,16,16,256]{3,2,1,0:T(8,128)S(1)} %slice.945, f32[8,18,16,256]{3,2,1,0:T(8,128)S(1)} %get-tuple-element.11, f32[8,18,16,256]{3,2,1,0:T(8,128)S(1)} %get-tuple-element.12, f32[8,18,16,256]{3,2,1,0:T(8,128)S(1)} %slice.938, f32[8,18,16,256]{3,2,1,0:T(8,128)S(1)} %slice.934, ...), kind=kLoop, calls=%fused_computation.212 | loop fusion | flops 15204352 | bytes 19398720 | tf_op jit(solution)/shard_map/mul | solution.py:158
  115.1 1.9 %collective-permute-start.4 = (f32[8,5,16,256]{3,2,1,0:T(8,128)S(1)}, f32[8,5,16,256]{3,2,1,0:T(8,128)S(1)}, u32[]{:S(2)}, u32[]{:S(2)}) collective-permute-start(f32[8,5,16,256]{3,2,1,0:T(8,128)S(1)} %get-tuple-element.41), channel_id=1, source_target_pairs={{0,1},{1,2},{2,3},{3,4},{4,5},{5,6},{6,7},{8,9},{9,10},{10,11},{11... | collective-permute-start | bytes 1966088 | tf_op jit(solution)/shard_map/ppermute | solution.py:21
  117.0 2.4 %collective-permute-start.5 = (f32[8,5,16,256]{3,2,1,0:T(8,128)S(1)}, f32[8,5,16,256]{3,2,1,0:T(8,128)S(1)}, u32[]{:S(2)}, u32[]{:S(2)}) collective-permute-start(f32[8,5,16,256]{3,2,1,0:T(8,128)S(1)} %get-tuple-element.42), channel_id=1, source_target_pairs={{1,0},{2,1},{3,2},{4,3},{5,4},{6,5},{7,6},{9,8},{10,9},{11,10},{12... | collective-permute-start | bytes 1966088 | tf_op jit(solution)/shard_map/ppermute | solution.py:23
  119.5 5.1 %collective-permute-done.4 = f32[8,5,16,256]{3,2,1,0:T(8,128)S(1)} collective-permute-done((f32[8,5,16,256]{3,2,1,0:T(8,128)S(1)}, f32[8,5,16,256]{3,2,1,0:T(8,128)S(1)}, u32[]{:S(2)}, u32[]{:S(2)}) %collective-permute-start.4) | collective-permute-done | bytes 655392 | tf_op jit(solution)/shard_map/ppermute | solution.py:21
  124.5 7.6 %collective-permute-done.5 = f32[8,5,16,256]{3,2,1,0:T(8,128)S(1)} collective-permute-done((f32[8,5,16,256]{3,2,1,0:T(8,128)S(1)}, f32[8,5,16,256]{3,2,1,0:T(8,128)S(1)}, u32[]{:S(2)}, u32[]{:S(2)}) %collective-permute-start.5) | collective-permute-done | bytes 655392 | tf_op jit(solution)/shard_map/ppermute | solution.py:23
  135.0 2.0 %slice.953 = f32[8,24,16,256]{3,2,1,0:T(8,128)} slice(f32[8,26,16,256]{3,2,1,0:T(8,128)S(1)} %get-tuple-element.28), slice={[0:8], [1:25], [0:16], [0:256]} | slice | bytes 6291456 | tf_op jit(solution)/shard_map/slice | solution.py:92
  137.0 10.4 %add_multiply_fusion = (f32[8,24,16,256]{3,2,1,0:T(8,128)S(1)}, f32[8,24,16,256]{3,2,1,0:T(8,128)}) fusion(f32[24]{0:T(128)S(1)} %slice.724, f32[8,26,16,256]{3,2,1,0:T(8,128)S(1)} %get-tuple-element.28, f32[8,24,16,256]{3,2,1,0:T(8,128)} %slice.953, f32[24,16,256]{2,1,0:T(8,128)} %copy-done.60, f32[24,16,256]{2,1,0:T(8,128)} %copy-done.62, ...), kind=kLoop, calls=%fused_computation.60 | loop fusion | flops 18874368 | bytes 24379488 | tf_op jit(solution)/shard_map/mul | solution.py:147
  149.6 6.0 %add_multiply_fusion.1 = (f32[8,22,16,256]{3,2,1,0:T(8,128)S(1)}, f32[8,22,16,256]{3,2,1,0:T(8,128)}) fusion(f32[22]{0:T(128)S(1)} %slice.742, f32[8,24,16,256]{3,2,1,0:T(8,128)S(1)} %get-tuple-element.9, f32[8,22,16,256]{3,2,1,0:T(8,128)S(1)} %slice.957, f32[22,16,256]{2,1,0:T(8,128)S(1)} %get-tuple-element.70, f32[22,16,256]{2,1,0:T(8,128)} %copy-done.18, ...), kind=kLoop, calls=%fused_computation.100 | loop fusion | flops 17301504 | bytes 22347864 | tf_op jit(solution)/shard_map/mul | solution.py:147
  157.9 3.3 %add_multiply_fusion.3 = (f32[8,20,16,256]{3,2,1,0:T(8,128)S(1)}, f32[8,20,16,256]{3,2,1,0:T(8,128)S(1)}) fusion(f32[20]{0:T(128)S(1)} %slice.760, f32[8,22,16,256]{3,2,1,0:T(8,128)S(1)} %get-tuple-element.7, f32[8,20,16,256]{3,2,1,0:T(8,128)S(1)} %slice.963, f32[20,16,256]{2,1,0:T(8,128)S(1)} %copy-done.26, f32[20,16,256]{2,1,0:T(8,128)S(1)} %copy-done.32, ...), kind=kLoop, calls=%fused_computation.140 | loop fusion | flops 15728640 | bytes 20316240 | tf_op jit(solution)/shard_map/mul | solution.py:147
  163.2 4.7 %fusion.110 = f32[8,18,16,256]{3,2,1,0:T(8,128)S(1)} fusion(f32[8,18,16,256]{3,2,1,0:T(8,128)S(1)} %slice.970, f32[8,20,16,256]{3,2,1,0:T(8,128)S(1)} %get-tuple-element.5, f32[8,20,16,256]{3,2,1,0:T(8,128)S(1)} %get-tuple-element.6, f32[8,20,16,256]{3,2,1,0:T(8,128)S(1)} %slice.963, f32[8,20,16,256]{3,2,1,0:T(8,128)S(1)} %slice.959, ...), kind=kLoop, calls=%fused_computation.175 | loop fusion | flops 16515072 | bytes 20643912 | tf_op jit(solution)/shard_map/add | solution.py:150
  170.1 3.8 %fusion.149 = f32[2,16,16,256]{3,2,1,0:T(8,128)S(1)} fusion(f32[4,2,16,16,256]{4,3,2,1,0:T(8,128)S(1)} %slice.974, f32[4,2,18,16,256]{4,3,2,1,0:T(8,128)S(1)} %bitcast.73, f32[4,16,16,256]{3,2,1,0:T(8,128)S(1)} %copy-done.8, f32[4,16,16,256]{3,2,1,0:T(8,128)S(1)} %copy-done.6, f32[4,16,16,256]{3,2,1,0:T(8,128)S(1)} %copy-done.10, ...), kind=kLoop, calls=%fused_computation.225 | loop fusion | flops 9306112 | bytes 13107200 | tf_op jit(solution)/shard_map/reduce_sum | solution.py:163
  (218 shorter events, 46.9 us)
Async XLA Ops:
  6.5 7.2 %copy-start.71 = (f32[2,16,16,256]{3,2,1,0:T(8,128)S(1)}, f32[2,16,16,256]{3,2,1,0:T(8,128)}, u32[]{:S(2)}) copy-start(f32[2,16,16,256]{3,2,1,0:T(8,128)} %param.7) | copy-start | bytes 1572868
  6.5 33.5 %all-gather.3.cloned.1.call-start = ((), (), s32[]{:S(2)}) async-start(), calls=%async_computation | async-start | bytes 1313280 | tf_op jit(solution)/shard_map/all_gather | solution.py:109
  42.0 10.8 %collective-permute-start = (f32[7,5,16,256]{3,2,1,0:T(8,128)S(1)}, f32[7,5,16,256]{3,2,1,0:T(8,128)S(1)}, u32[]{:S(2)}, u32[]{:S(2)}) collective-permute-start(f32[7,5,16,256]{3,2,1,0:T(8,128)S(1)} %get-tuple-element.47), channel_id=1, source_target_pairs={{0,1},{1,2},{2,3},{3,4},{4,5},{5,6},{6,7},{8,9},{9,10},{10,11},{11... | collective-permute-start | bytes 1720328 | tf_op jit(solution)/shard_map/ppermute | solution.py:21
  46.1 14.4 %collective-permute-start.1 = (f32[7,5,16,256]{3,2,1,0:T(8,128)S(1)}, f32[7,5,16,256]{3,2,1,0:T(8,128)S(1)}, u32[]{:S(2)}, u32[]{:S(2)}) collective-permute-start(f32[7,5,16,256]{3,2,1,0:T(8,128)S(1)} %get-tuple-element.48), channel_id=1, source_target_pairs={{1,0},{2,1},{3,2},{4,3},{5,4},{6,5},{7,6},{9,8},{10,9},{11,10},{12... | collective-permute-start | bytes 1720328 | tf_op jit(solution)/shard_map/ppermute | solution.py:23
  61.0 7.2 %copy-start.33 = (f32[20,16,256]{2,1,0:T(8,128)}, f32[20,16,256]{2,1,0:T(8,128)S(1)}, u32[]{:S(2)}) copy-start(f32[20,16,256]{2,1,0:T(8,128)S(1)} %get-tuple-element.32) | copy-start | bytes 983044
  61.0 7.2 %copy-start.36 = (f32[20,16,256]{2,1,0:T(8,128)}, f32[20,16,256]{2,1,0:T(8,128)S(1)}, u32[]{:S(2)}) copy-start(f32[20,16,256]{2,1,0:T(8,128)S(1)} %get-tuple-element.33) | copy-start | bytes 983044
  61.1 4.9 %copy-start.19 = (f32[22,16,256]{2,1,0:T(8,128)}, f32[22,16,256]{2,1,0:T(8,128)S(1)}, u32[]{:S(2)}) copy-start(f32[22,16,256]{2,1,0:T(8,128)S(1)} %get-tuple-element.35) | copy-start | bytes 1081348
  61.1 4.9 %copy-start.20 = (f32[22,16,256]{2,1,0:T(8,128)}, f32[22,16,256]{2,1,0:T(8,128)S(1)}, u32[]{:S(2)}) copy-start(f32[22,16,256]{2,1,0:T(8,128)S(1)} %get-tuple-element.36) | copy-start | bytes 1081348
  65.0 5.1 %copy-start.39 = (f32[18,16,256]{2,1,0:T(8,128)}, f32[18,16,256]{2,1,0:T(8,128)S(1)}, u32[]{:S(2)}) copy-start(f32[18,16,256]{2,1,0:T(8,128)S(1)} %get-tuple-element.25) | copy-start | bytes 884740
  65.0 5.1 %copy-start.42 = (f32[18,16,256]{2,1,0:T(8,128)}, f32[18,16,256]{2,1,0:T(8,128)S(1)}, u32[]{:S(2)}) copy-start(f32[18,16,256]{2,1,0:T(8,128)S(1)} %get-tuple-element.26) | copy-start | bytes 884740
  65.2 4.9 %copy-start.45 = (f32[18,16,256]{2,1,0:T(8,128)}, f32[18,16,256]{2,1,0:T(8,128)S(1)}, u32[]{:S(2)}) copy-start(f32[18,16,256]{2,1,0:T(8,128)S(1)} %get-tuple-element.77) | copy-start | bytes 884740
  65.2 4.9 %copy-start.48 = (f32[18,16,256]{2,1,0:T(8,128)}, f32[18,16,256]{2,1,0:T(8,128)S(1)}, u32[]{:S(2)}) copy-start(f32[18,16,256]{2,1,0:T(8,128)S(1)} %get-tuple-element.78) | copy-start | bytes 884740
  65.3 4.9 %copy-start.51 = (f32[18,16,256]{2,1,0:T(8,128)}, f32[18,16,256]{2,1,0:T(8,128)S(1)}, u32[]{:S(2)}) copy-start(f32[18,16,256]{2,1,0:T(8,128)S(1)} %get-tuple-element.79) | copy-start | bytes 884740
  65.3 4.9 %copy-start.53 = (f32[18,16,256]{2,1,0:T(8,128)}, f32[18,16,256]{2,1,0:T(8,128)S(1)}, u32[]{:S(2)}) copy-start(f32[18,16,256]{2,1,0:T(8,128)S(1)} %get-tuple-element.80) | copy-start | bytes 884740
  73.7 6.4 %copy-start.72 = (f32[16,16,256]{2,1,0:T(8,128)S(1)}, f32[16,16,256]{2,1,0:T(8,128)}, u32[]{:S(2)}) copy-start(f32[16,16,256]{2,1,0:T(8,128)} %param.11) | copy-start | bytes 786436
  75.7 8.0 %collective-permute-start.2 = (f32[8,4,16,256]{3,2,1,0:T(8,128)S(1)}, f32[8,4,16,256]{3,2,1,0:T(8,128)S(1)}, u32[]{:S(2)}, u32[]{:S(2)}) collective-permute-start(f32[8,4,16,256]{3,2,1,0:T(8,128)S(1)} %get-tuple-element.43), channel_id=1, source_target_pairs={{0,1},{1,2},{2,3},{3,4},{4,5},{5,6},{6,7},{8,9},{9,10},{10,11},{11... | collective-permute-start | bytes 1572872 | tf_op jit(solution)/shard_map/ppermute | solution.py:21
  77.6 13.3 %collective-permute-start.3 = (f32[8,4,16,256]{3,2,1,0:T(8,128)S(1)}, f32[8,4,16,256]{3,2,1,0:T(8,128)S(1)}, u32[]{:S(2)}, u32[]{:S(2)}) collective-permute-start(f32[8,4,16,256]{3,2,1,0:T(8,128)S(1)} %get-tuple-element.44), channel_id=1, source_target_pairs={{1,0},{2,1},{3,2},{4,3},{5,4},{6,5},{7,6},{9,8},{10,9},{11,10},{12... | collective-permute-start | bytes 1572872 | tf_op jit(solution)/shard_map/ppermute | solution.py:23
  106.2 3.5 %copy-start.66 = (f32[16,16,256]{2,1,0:T(8,128)S(1)}, f32[16,16,256]{2,1,0:T(8,128)}, u32[]{:S(2)}) copy-start(f32[16,16,256]{2,1,0:T(8,128)} %get-tuple-element.87) | copy-start | bytes 786436
  106.2 3.5 %copy-start.67 = (f32[16,16,256]{2,1,0:T(8,128)S(1)}, f32[16,16,256]{2,1,0:T(8,128)}, u32[]{:S(2)}) copy-start(f32[16,16,256]{2,1,0:T(8,128)} %get-tuple-element.45) | copy-start | bytes 786436
  106.2 3.6 %copy-start.68 = (f32[16,16,256]{2,1,0:T(8,128)S(1)}, f32[16,16,256]{2,1,0:T(8,128)}, u32[]{:S(2)}) copy-start(f32[16,16,256]{2,1,0:T(8,128)} %get-tuple-element.46) | copy-start | bytes 786436
  115.1 9.4 %collective-permute-start.4 = (f32[8,5,16,256]{3,2,1,0:T(8,128)S(1)}, f32[8,5,16,256]{3,2,1,0:T(8,128)S(1)}, u32[]{:S(2)}, u32[]{:S(2)}) collective-permute-start(f32[8,5,16,256]{3,2,1,0:T(8,128)S(1)} %get-tuple-element.41), channel_id=1, source_target_pairs={{0,1},{1,2},{2,3},{3,4},{4,5},{5,6},{6,7},{8,9},{9,10},{10,11},{11... | collective-permute-start | bytes 1966088 | tf_op jit(solution)/shard_map/ppermute | solution.py:21
  117.0 15.1 %collective-permute-start.5 = (f32[8,5,16,256]{3,2,1,0:T(8,128)S(1)}, f32[8,5,16,256]{3,2,1,0:T(8,128)S(1)}, u32[]{:S(2)}, u32[]{:S(2)}) collective-permute-start(f32[8,5,16,256]{3,2,1,0:T(8,128)S(1)} %get-tuple-element.42), channel_id=1, source_target_pairs={{1,0},{2,1},{3,2},{4,3},{5,4},{6,5},{7,6},{9,8},{10,9},{11,10},{12... | collective-permute-start | bytes 1966088 | tf_op jit(solution)/shard_map/ppermute | solution.py:23
  163.2 4.9 %copy-start.12 = (f32[4,16,16,256]{3,2,1,0:T(8,128)S(1)}, f32[4,16,16,256]{3,2,1,0:T(8,128)}, u32[]{:S(2)}) copy-start(f32[4,16,16,256]{3,2,1,0:T(8,128)} %copy-done.11) | copy-start | bytes 3145732
  170.1 3.8 %copy-start.70 = (f32[16,16,256]{2,1,0:T(8,128)S(1)}, f32[16,16,256]{2,1,0:T(8,128)}, u32[]{:S(2)}) copy-start(f32[16,16,256]{2,1,0:T(8,128)} %get-tuple-element.81) | copy-start | bytes 786436
  (56 other events, 96.9 us)
Sparse Core Ops, SparseCore 0:
  10.4 29.5 all-gather.2
